TPU v7x, 256 devices: a whole 4x4x8 slice. The times are simulated.
256 devices in a mesh: seq: 64 (over y, z, core), head: 4 (over x).
Axes of the slice: x: 4, y: 4, z: 8, core: 2. Of those that a mesh axis runs over, the one named last changes fastest.
Arguments:
- queries: bfloat16 [32768, 4096], P(('seq', 'head')), may hold values from -6 to 6
- keys: bfloat16 [32768, 4096], P(('seq', 'head')), may hold values from -6 to 6
- values: bfloat16 [32768, 4096], P(('seq', 'head')), may hold values from -6 to 6
- cluster_ids: int32 [32, 32768, 1], P(None, 'seq'), may hold values from 0 to 127; in each aligned block of 128 rows (0 to 127, 128 to 255, ..., all dimensions but the last counted through in order) at most 2 rows name the same one
- out_weight: bfloat16 [4096, 4096], P('head', 'seq'), may hold values from -0.09375 to 0.09375
Outputs:
- projected: bfloat16 [32768, 4096], P('seq', 'head')
Inputs may be any that keep to these rules, and one draw needn't show every extreme that they name: `cluster_ids`: in each aligned block of 128 tokens of one head (the rows of one device), no cluster id appears more than 2 times, and some cluster appears exactly 2 times.
All inputs are finite; a program needn't handle non-finite values.
Results may differ from a plain program's by a relative error of at most 0.014.
Values may be sent and summed in bfloat16 or wider, within the bound.
No kernel may reach another device: no remote copies, remote signals or barrier semaphores. Data moves between devices by JAX's collectives and lax.ppermute only.
A program may use at most 128 MiB of HBM per device.

v0:
```python
import jax
import jax.numpy as jnp
from jax import lax
from jax.sharding import PartitionSpec as P

HEADS = 32
HD = 128
CLUSTERS = 128


def slot_table(block_ids, slot_depth):
    sub_rows = block_ids.shape[-1]
    onehot = (block_ids[..., None] == jnp.arange(CLUSTERS, dtype=jnp.int32)).astype(jnp.float32)
    lower = (jnp.arange(sub_rows)[:, None] >= jnp.arange(sub_rows)[None, :]).astype(jnp.float32)
    running = jnp.einsum("ts,abse->abte", lower, onehot)
    ranking = (jnp.sum(running * onehot, axis=-1) - 1.0).astype(jnp.int32)
    depth_hit = (ranking[..., None] == jnp.arange(slot_depth, dtype=jnp.int32)).astype(jnp.bfloat16)
    return onehot.astype(jnp.bfloat16)[..., :, None] * depth_hit[..., None, :]


def attend_blocks(packed, validity):
    scores = jnp.einsum(
        "cqd,ckd->cqk", packed[0], packed[1], preferred_element_type=jnp.float32
    ) * HD ** (-0.5)
    scores = jnp.where(validity[:, None, :], scores, -1e30)
    row_max = jnp.max(scores, axis=-1, keepdims=True)
    raised = jnp.exp(scores - row_max)
    weights = (raised / jnp.sum(raised, axis=-1, keepdims=True)).astype(jnp.bfloat16)
    return jnp.einsum(
        "cqk,ckd->cqd", weights, packed[2], preferred_element_type=jnp.float32
    ).astype(jnp.bfloat16)


def body(queries, keys, values, cluster_ids, out_weight):
    n_seq = lax.axis_size("seq")
    n_head = lax.axis_size("head")
    head_group = lax.axis_index("head")
    tok_dev = cluster_ids.shape[1]
    sub_rows = tok_dev // n_head
    group_heads = HEADS // n_head
    slot_depth = max(2, 2 * tok_dev // (n_head * CLUSTERS))
    per_owner = group_heads * CLUSTERS // n_seq
    n_src = n_seq * n_head
    all_ids = cluster_ids[:, :, 0]
    own_ids = lax.dynamic_slice_in_dim(all_ids, head_group * sub_rows, sub_rows, 1)
    own_table = slot_table(own_ids[:, None, :], slot_depth)[:, 0]
    stacked = jnp.stack([t.reshape(sub_rows, HEADS, HD) for t in (queries, keys, values)])
    packed = jnp.einsum(
        "htcr,xthd->xhcrd", own_table, stacked, preferred_element_type=jnp.float32
    ).astype(jnp.bfloat16)
    packed = packed.reshape(3, n_head, per_owner, n_seq, slot_depth, HD)
    packed = packed.transpose(0, 3, 1, 2, 4, 5).reshape(3, n_src, per_owner, slot_depth, HD)
    arrived = lax.all_to_all(packed, ("seq", "head"), split_axis=1, concat_axis=1, tiled=True)
    arrived = arrived.transpose(0, 2, 1, 3, 4).reshape(3, per_owner, n_src * slot_depth, HD)
    group_ids = lax.dynamic_slice_in_dim(all_ids, head_group * group_heads, group_heads, 0)
    seen_ids = lax.all_gather(group_ids, "seq", axis=1, tiled=True)
    seen_ids = seen_ids.reshape(group_heads, n_src, sub_rows)
    owned = jnp.arange(CLUSTERS // n_seq, dtype=jnp.int32) * n_seq + lax.axis_index("seq")
    counts = jnp.sum(
        (seen_ids[:, None, :, :] == owned[None, :, None, None]).astype(jnp.int32), axis=-1
    )
    counts = counts.reshape(per_owner, n_src)
    valid = counts[:, :, None] > jnp.arange(slot_depth, dtype=jnp.int32)
    valid = valid.reshape(per_owner, n_src * slot_depth)
    result_block = attend_blocks(arrived, valid)
    result_block = result_block.reshape(per_owner, n_seq, n_head * slot_depth, HD)
    returned = lax.all_to_all(result_block, "seq", split_axis=1, concat_axis=1, tiled=True)
    returned = returned.reshape(group_heads, CLUSTERS, n_head, slot_depth, HD)
    group_ids = group_ids.reshape(group_heads, n_head, sub_rows)
    home_table = slot_table(group_ids, slot_depth)
    gathered = jnp.einsum(
        "hltcr,hclrd->lthd", home_table, returned, preferred_element_type=jnp.float32
    ).astype(jnp.bfloat16)
    gathered = gathered.reshape(tok_dev, group_heads * HD)
    partial_value = jnp.dot(
        gathered,
        lax.all_gather(out_weight, "seq", axis=1, tiled=True),
        preferred_element_type=jnp.float32,
    )
    return lax.psum_scatter(
        partial_value.astype(jnp.bfloat16), "head", scatter_dimension=1, tiled=True
    )


def solution(mesh):
    in_specs = (
        P(("seq", "head"), None),
        P(("seq", "head"), None),
        P(("seq", "head"), None),
        P(None, "seq", None),
        P("head", "seq"),
    )
    out_specs = P("seq", "head")
    return jax.shard_map(body, mesh=mesh, in_specs=in_specs, out_specs=out_specs, check_vma=False)
```

profile of v0, /device:TPU:1, one launch (start us, length us, event | category | flops | bytes accessed | tf_op | source)
XLA Modules:
  0.0 354.4 jit_solution(14528924154040969133)
XLA Ops:
  6.5 0.8 copy-done
  7.4 1.3 convert_convert_fusion.1
  8.7 0.7 fusion.11
  9.4 0.7 copy.67
  10.1 1.3 copy.70
  11.4 0.7 copy.68
  12.1 1.3 copy.71
  13.4 0.7 copy.69
  14.0 1.3 copy.72
  15.4 3.3 convert_bitcast_fusion
  18.7 2.6 copy.73
  21.3 4.0 %copy.74 = bf16[3,64,4,16,2,128]{5,3,4,2,1,0:T(8,128)(2,1)S(1)} copy(bf16[3,64,4,16,2,128]{5,1,3,2,4,0:T(8,128)(2,1)S(1)} %bitcast.66) | data formatting | bytes 12582912 | tf_op jit(solution)/shard_map/transpose | solution.py:52
  25.4 3.7 %copy.75 = bf16[3,256,16,2,128]{4,2,3,0,1:T(8,128)(2,1)} copy(bf16[3,256,16,2,128]{4,2,3,1,0:T(8,128)(2,1)S(1)} %bitcast.67) | data formatting | bytes 12582912 | tf_op jit(solution)/shard_map/reshape | solution.py:52
  29.1 16.5 %all-to-all-start = ((bf16[3,256,16,2,128]{4,2,3,0,1:T(8,128)(2,1)}), bf16[3,256,16,2,128]{4,2,3,0,1:T(8,128)(2,1)}, u32[]{:S(2)}, u32[]{:S(2)}) async-start(bf16[3,256,16,2,128]{4,2,3,0,1:T(8,128)(2,1)} %copy.75), calls=%async_computation | async-start | bytes 12582912 | tf_op jit(solution)/shard_map/all_to_all | solution.py:53
  45.6 0.0 all-gather.6.cloned.1.call-start
  45.7 0.6 copy.105
  46.3 0.1 all-gather.6.cloned.1.call-update
  46.4 0.0 all-gather.4.cloned.1.call-start
  46.4 0.7 all-gather.4.cloned.1.call-update
  47.2 0.1 gt.29
  47.3 91.2 %all-gather.6.cloned.1.call-done = s32[8,32768,1]{1,0,2:T(8,128)} async-done(((s32[8,512,1]{1,0,2:T(8,128)}), s32[8,32768,1]{1,0,2:T(8,128)}) %all-gather.6.cloned.1.call-update) | async-done | bytes 1048592 | tf_op jit(solution)/shard_map/all_gather | solution.py:56
  138.5 1.4 copy.64
  140.0 0.7 convert_reduce_fusion
  140.7 0.1 copy.65
  140.8 0.1 gt.26
  140.9 0.1 broadcast_compare_fusion
  141.0 0.1 copy.66
  141.2 56.2 %all-to-all-done = bf16[3,256,16,2,128]{4,2,3,0,1:T(8,128)(2,1)} async-done(((bf16[3,256,16,2,128]{4,2,3,0,1:T(8,128)(2,1)}), bf16[3,256,16,2,128]{4,2,3,0,1:T(8,128)(2,1)}, u32[]{:S(2)}, u32[]{:S(2)}) %all-to-all-start) | async-done | bytes 6291488 | tf_op jit(solution)/shard_map/all_to_all | solution.py:53
  197.4 4.5 %fusion.45 = (bf16[1,16,256,2,128]{4,1,3,0,2:T(8,128)(2,1)S(1)}, bf16[1,16,256,2,128]{4,1,3,0,2:T(8,128)(2,1)S(1)}, bf16[1,16,256,2,128]{4,1,3,0,2:T(8,128)(2,1)S(1)}) fusion(bf16[3,16,256,2,128]{4,1,3,0,2:T(8,128)(2,1)} %bitcast.17), kind=kLoop, calls=%fused_computation.60 | loop fusion | bytes 12582912 | tf_op jit(solution)/shard_map/slice | solution.py:23
  201.9 2.0 copy.76
  203.9 3.2 copy.77
  207.2 3.2 copy.78
  210.4 9.8 %fusion.46 = (f32[16,512]{1,0:T(8,128)S(1)}, f32[16,512,512]{1,2,0:T(8,128)}) fusion(pred[16,512]{1,0:T(8,128)(4,1)S(1)} %copy.66, bf16[16,512,128]{2,1,0:T(8,128)(2,1)S(1)} %bitcast.71, bf16[16,512,128]{2,1,0:T(8,128)(2,1)} %bitcast.72), kind=kOutput, calls=%fused_computation.61 | convolution fusion | flops 1090519552 | bytes 21012480 | tf_op jit(solution)/shard_map/sub | solution.py:27
  220.2 9.3 %convert_bitcast_fusion.1 = bf16[16,64,8,128]{3,2,1,0:T(8,128)(2,1)S(1)} fusion(bf16[16,512,128]{2,1,0:T(8,128)(2,1)} %bitcast.73, f32[16,512,512]{1,2,0:T(8,128)} %get-tuple-element.11, f32[16,512]{1,0:T(8,128)S(1)} %get-tuple-element.10), kind=kOutput, calls=%fused_computation.28 | convolution fusion | flops 1083179008 | bytes 21004288 | tf_op jit(solution)/shard_map/cqk,ckd->cqd/dot_general | solution.py:29
  229.5 3.8 %copy.80 = bf16[16,64,8,128]{3,0,2,1:T(8,128)(2,1)} copy(bf16[16,64,8,128]{3,2,1,0:T(8,128)(2,1)S(1)} %convert_bitcast_fusion.1) | data formatting | bytes 4194304 | tf_op jit(solution)/shard_map/reshape | solution.py:66
  233.3 5.4 %all-to-all-start.1 = ((bf16[16,64,8,128]{3,0,2,1:T(8,128)(2,1)}), bf16[16,64,8,128]{3,0,2,1:T(8,128)(2,1)S(1)}, u32[]{:S(2)}, u32[]{:S(2)}) async-start(bf16[16,64,8,128]{3,0,2,1:T(8,128)(2,1)} %copy.80), calls=%async_computation.1 | async-start | bytes 4194304 | tf_op jit(solution)/shard_map/all_to_all | solution.py:67
  238.7 0.0 reduce-scatter.2.cloned.1.call-start
  238.8 0.3 convert_convert_fusion
  239.0 1.6 copy.82
  240.6 0.7 fusion.12
  241.3 48.7 %all-to-all-done.1 = bf16[16,64,8,128]{3,0,2,1:T(8,128)(2,1)S(1)} async-done(((bf16[16,64,8,128]{3,0,2,1:T(8,128)(2,1)}), bf16[16,64,8,128]{3,0,2,1:T(8,128)(2,1)S(1)}, u32[]{:S(2)}, u32[]{:S(2)}) %all-to-all-start.1) | async-done | bytes 2097184 | tf_op jit(solution)/shard_map/all_to_all | solution.py:67
  290.1 1.4 copy.81
  291.4 2.6 fusion.25
  294.0 0.7 copy.84
  294.7 0.0 all-gather.4.cloned.1.call-done
  294.8 9.5 %convolution_convert_fusion = bf16[512,4096]{1,0:T(8,128)(2,1)} fusion(bf16[1024,4096]{0,1:T(8,128)(2,1)} %all-gather.4.cloned.1.call-done, bf16[64,8,8,128]{3,2,1,0:T(8,128)(2,1)S(1)} %bitcast.77), kind=kOutput, calls=%fused_computation.10 | convolution fusion | flops 4297064448 | bytes 13631488 | tf_op jit(solution)/shard_map/dot_general | solution.py:75
  304.3 0.0 reduce-scatter.2.cloned.1.call-update
  304.3 43.5 %reduce-scatter.2.cloned.1.call-done = bf16[512,1024]{1,0:T(8,128)(2,1)} async-done(((bf16[512,4096]{1,0:T(8,128)(2,1)}), bf16[512,1024]{1,0:T(8,128)(2,1)}) %reduce-scatter.2.cloned.1.call-update) | async-done | bytes 1048592 | tf_op jit(solution)/shard_map/reduce_scatter | solution.py:80
  (26 shorter events, 0.1 us)
Async XLA Ops:
  6.5 0.8 copy-start
  6.5 2.8 copy-start.2
  9.4 2.0 copy-start.3
  11.4 2.0 copy-start.4
  13.4 2.0 copy-start.5
  14.0 1.3 copy-start.7
  29.1 168.3 %all-to-all-start = ((bf16[3,256,16,2,128]{4,2,3,0,1:T(8,128)(2,1)}), bf16[3,256,16,2,128]{4,2,3,0,1:T(8,128)(2,1)}, u32[]{:S(2)}, u32[]{:S(2)}) async-start(bf16[3,256,16,2,128]{4,2,3,0,1:T(8,128)(2,1)} %copy.75), calls=%async_computation | async-start | bytes 12582912 | tf_op jit(solution)/shard_map/all_to_all | solution.py:53
  45.6 92.9 %all-gather.6.cloned.1.call-start = ((), (), s32[]{:S(2)}) async-start(), calls=%async_computation.5 | async-start | bytes 1064960 | tf_op jit(solution)/shard_map/all_gather | solution.py:56
  46.4 248.4 %all-gather.4.cloned.1.call-start = ((), (), s32[]{:S(2)}) async-start(), calls=%async_computation.3 | async-start | bytes 8519680 | tf_op jit(solution)/shard_map/all_gather | solution.py:77
  233.3 5.5 %copy-start.8 = (s32[8,512,1]{1,0,2:T(8,128)S(1)}, s32[8,512,1]{1,0,2:T(8,128)}, u32[]{:S(2)}) copy-start(s32[8,512,1]{1,0,2:T(8,128)} %copy.105) | copy-start | bytes 49156
  233.3 56.8 %all-to-all-start.1 = ((bf16[16,64,8,128]{3,0,2,1:T(8,128)(2,1)}), bf16[16,64,8,128]{3,0,2,1:T(8,128)(2,1)S(1)}, u32[]{:S(2)}, u32[]{:S(2)}) async-start(bf16[16,64,8,128]{3,0,2,1:T(8,128)(2,1)} %copy.80), calls=%async_computation.1 | async-start | bytes 4194304 | tf_op jit(solution)/shard_map/all_to_all | solution.py:67
  238.7 109.1 %reduce-scatter.2.cloned.1.call-start = ((), (), s32[]{:S(2)}) async-start(), calls=%async_computation.4 | async-start | bytes 5242880 | tf_op jit(solution)/shard_map/reduce_scatter | solution.py:80
  241.3 50.1 %copy-start.6 = (bf16[8,4,128,128]{3,2,0,1:T(8,128)(2,1)S(1)}, bf16[8,4,128,128]{3,2,0,1:T(8,128)(2,1)}, u32[]{:S(2)}) copy-start(bf16[8,4,128,128]{3,2,0,1:T(8,128)(2,1)} %copy.82) | copy-start | bytes 3145732
  304.3 43.6 %copy-start.1 = (s32[32,512,1]{1,2,0:T(1,128)S(1)}, s32[32,512,1]{1,2,0:T(1,128)}, u32[]{:S(2)}) copy-start(s32[32,512,1]{1,2,0:T(1,128)} %param.8) | copy-start | bytes 196612
Sparse Core Ops, SparseCore 0:
  49.3 89.2 all-gather.5
  141.3 91.9 all-gather.3
  304.4 43.3 reduce-scatter.1
where the time goes:
time: 355 us; the launch traced here: 354 us
  waiting for transfers between devices  241 us (68%)
  local copies, waits for them, and re-layouts  40.2 us (11%)
  matrix products  35.8 us (10%)
  starting transfers between devices  22.1 us (6%)
  between operations  13.4 us (4%)
    all_gather x1, waiting for transfers between devices, body(): seen_ids = lax.all_gather(group_ids, 'seq', axis=1, tiled=True)  91.2 us
    all_to_all x1, waiting for transfers between devices, body(): lax.all_to_all(packed, ('seq', 'head'), split_axis=1, concat_axis=1, tile...  56.2 us
    all_to_all x1, waiting for transfers between devices, body(): lax.all_to_all(result_block, 'seq', split_axis=1, concat_axis=1, tiled=True)  48.7 us
    reduce_scatter x1, waiting for transfers between devices, body(): lax.psum_scatter(partial_value.astype(jnp.bfloat16), 'head', scatter_dime...  43.5 us
    all_to_all x1, starting transfers between devices, body(): lax.all_to_all(packed, ('seq', 'head'), split_axis=1, concat_axis=1, tile...  16.5 us
    sub x1, matrix products, attend_blocks(): raised = jnp.exp(scores - row_max)  9.82 us
    dot_general x1, matrix products, body(): jnp.dot(gathered, lax.all_gather(out_weight, 'seq', axis=1, tiled=True),...  9.5 us
    dot_general x1, matrix products, attend_blocks(): jnp.einsum('cqk,ckd->cqd', weights, packed[2], preferred_element_type=jnp...  9.25 us
  transfers between devices with their start and end apart: 5, of which 4 were waited for; matrix products, arithmetic and copies ran while one was open for 13% of the time, Pallas kernels for 0%

commit v1 on v0

--- a/solution.py
+++ b/solution.py
@@ -53,7 +53,9 @@
     arrived = lax.all_to_all(packed, ("seq", "head"), split_axis=1, concat_axis=1, tiled=True)
     arrived = arrived.transpose(0, 2, 1, 3, 4).reshape(3, per_owner, n_src * slot_depth, HD)
     group_ids = lax.dynamic_slice_in_dim(all_ids, head_group * group_heads, group_heads, 0)
-    seen_ids = lax.all_gather(group_ids, "seq", axis=1, tiled=True)
+    seen_ids = jnp.concatenate(
+        lax.all_to_all(jnp.stack([group_ids] * lax.axis_size("seq")), "seq", 0, 0), axis=1
+    )
     seen_ids = seen_ids.reshape(group_heads, n_src, sub_rows)
     owned = jnp.arange(CLUSTERS // n_seq, dtype=jnp.int32) * n_seq + lax.axis_index("seq")
     counts = jnp.sum(

time: 355 us -> 385 us (1.085)
  waiting for transfers between devices: 241 us -> 267 us
  starting transfers between devices: 22.1 us -> 28 us
    all_to_all x1, waiting for transfers between devices: 56.2 us -> 166 us  [body(): lax.all_to_all(packed, ('seq', 'head'), split_axis=1, concat_axis=1, tile...]
    all_gather x1 -> x0, waiting for transfers between devices: 91.2 us -> none  [body(): seen_ids = lax.all_gather(group_ids, 'seq', axis=1, tiled=True)]
    all_to_all x0 -> x1, starting transfers between devices: none -> 13.2 us  [body(): lax.all_to_all(jnp.stack([group_ids] * lax.axis_size('seq')), 'seq', 0, 0)]
    all_to_all x0 -> x1, waiting for transfers between devices: none -> 8.32 us  [body(): lax.all_to_all(jnp.stack([group_ids] * lax.axis_size('seq')), 'seq', 0, 0)]
    all_to_all x1, starting transfers between devices: 16.5 us -> 9.57 us  [body(): lax.all_to_all(packed, ('seq', 'head'), split_axis=1, concat_axis=1, tile...]
  transfers between devices with their start and end apart: 5 -> 5, of which waited for: 4 -> 4; matrix products, arithmetic and copies ran while one was open for 13% -> 17% of each run, Pallas kernels for 0% -> 0%
where the time goes in v1:
time: 385 us; the launch traced here: 384 us
  waiting for transfers between devices  267 us (69%)
  local copies, waits for them, and re-layouts  40.4 us (10%)
  matrix products  34.1 us (9%)
  starting transfers between devices  28 us (7%)
  between operations  13.7 us (4%)
    all_to_all x1, waiting for transfers between devices, body(): lax.all_to_all(packed, ('seq', 'head'), split_axis=1, concat_axis=1, tile...  166 us
    all_to_all x1, waiting for transfers between devices, body(): lax.all_to_all(result_block, 'seq', split_axis=1, concat_axis=1, tiled=True)  48.8 us
    reduce_scatter x1, waiting for transfers between devices, body(): lax.psum_scatter(partial_value.astype(jnp.bfloat16), 'head', scatter_dime...  43.6 us
    all_to_all x1, starting transfers between devices, body(): lax.all_to_all(jnp.stack([group_ids] * lax.axis_size('seq')), 'seq', 0, 0)  13.2 us
    sub x1, matrix products, attend_blocks(): raised = jnp.exp(scores - row_max)  9.84 us
    all_to_all x1, starting transfers between devices, body(): lax.all_to_all(packed, ('seq', 'head'), split_axis=1, concat_axis=1, tile...  9.57 us
    dot_general x1, matrix products, body(): jnp.dot(gathered, lax.all_gather(out_weight, 'seq', axis=1, tiled=True),...  9.48 us
    dot_general x1, matrix products, attend_blocks(): jnp.einsum('cqk,ckd->cqd', weights, packed[2], preferred_element_type=jnp...  8.89 us
  transfers between devices with their start and end apart: 5, of which 4 were waited for; matrix products, arithmetic and copies ran while one was open for 17% of the time, Pallas kernels for 0%

profile of v1, /device:TPU:1, one launch (start us, length us, event | category | flops | bytes accessed | tf_op | source)
XLA Modules:
  0.0 384.5 jit_solution(870826962583269959)
XLA Ops:
  6.5 0.8 copy-done
  7.4 1.1 stack.7
  8.5 13.2 %all-to-all-start = ((s32[64,8,512]{2,1,0:T(8,128)}), s32[64,8,512]{2,1,0:T(8,128)S(1)}, u32[]{:S(2)}, u32[]{:S(2)}) async-start(s32[64,8,512]{2,1,0:T(8,128)} %stack.7), calls=%async_computation | async-start | bytes 2097152 | tf_op jit(solution)/shard_map/all_to_all | solution.py:57
  21.7 0.7 copy.65
  22.4 1.3 copy.68
  23.7 0.7 copy.66
  24.4 1.3 copy.69
  25.7 0.7 copy.67
  26.3 1.3 copy.70
  27.7 0.7 fusion.11
  28.4 0.3 convert_convert_fusion.1
  28.6 0.2 copy-done.5
  28.9 0.3 copy-done.6
  29.2 0.3 copy-done.7
  29.5 2.0 convert_bitcast_fusion
  31.5 2.6 copy.71
  34.1 4.0 %copy.72 = bf16[3,64,4,16,2,128]{5,3,4,2,1,0:T(8,128)(2,1)S(1)} copy(bf16[3,64,4,16,2,128]{5,1,3,2,4,0:T(8,128)(2,1)S(1)} %bitcast.68) | data formatting | bytes 12582912 | tf_op jit(solution)/shard_map/transpose | solution.py:52
  38.2 3.7 copy.73
  41.9 8.3 %all-to-all-done = s32[64,8,512]{2,1,0:T(8,128)S(1)} async-done(((s32[64,8,512]{2,1,0:T(8,128)}), s32[64,8,512]{2,1,0:T(8,128)S(1)}, u32[]{:S(2)}, u32[]{:S(2)}) %all-to-all-start) | async-done | bytes 1048608 | tf_op jit(solution)/shard_map/all_to_all | solution.py:57
  50.2 9.6 %all-to-all-start.1 = ((bf16[3,256,16,2,128]{4,2,3,0,1:T(8,128)(2,1)}), bf16[3,256,16,2,128]{4,2,3,0,1:T(8,128)(2,1)}, u32[]{:S(2)}, u32[]{:S(2)}) async-start(bf16[3,256,16,2,128]{4,2,3,0,1:T(8,128)(2,1)} %copy.73), calls=%async_computation.1 | async-start | bytes 12582912 | tf_op jit(solution)/shard_map/all_to_all | solution.py:53
  59.9 0.7 all-gather.2.cloned.1.call-update
  60.6 0.1 gt.29
  60.7 0.6 copy.62
  61.3 0.1 eq.105
  61.4 0.7 convert_reduce_fusion
  62.1 0.1 copy.63
  62.2 0.1 gt.26
  62.3 0.1 broadcast_compare_fusion
  62.5 0.1 copy.64
  62.6 165.5 %all-to-all-done.1 = bf16[3,256,16,2,128]{4,2,3,0,1:T(8,128)(2,1)} async-done(((bf16[3,256,16,2,128]{4,2,3,0,1:T(8,128)(2,1)}), bf16[3,256,16,2,128]{4,2,3,0,1:T(8,128)(2,1)}, u32[]{:S(2)}, u32[]{:S(2)}) %all-to-all-start.1) | async-done | bytes 6291488 | tf_op jit(solution)/shard_map/all_to_all | solution.py:53
  228.1 4.2 %fusion.45 = (bf16[1,16,256,2,128]{4,1,3,0,2:T(8,128)(2,1)S(1)}, bf16[1,16,256,2,128]{4,1,3,0,2:T(8,128)(2,1)S(1)}, bf16[1,16,256,2,128]{4,1,3,0,2:T(8,128)(2,1)S(1)}) fusion(bf16[3,16,256,2,128]{4,1,3,0,2:T(8,128)(2,1)} %bitcast.18), kind=kLoop, calls=%fused_computation.61 | loop fusion | bytes 12582912 | tf_op jit(solution)/shard_map/slice | solution.py:23
  232.3 2.0 copy.74
  234.3 3.2 copy.75
  237.5 3.3 copy.76
  240.8 9.8 %fusion.46 = (f32[16,512]{1,0:T(8,128)S(1)}, f32[16,512,512]{1,2,0:T(8,128)}) fusion(pred[16,512]{1,0:T(8,128)(4,1)S(1)} %copy.64, bf16[16,512,128]{2,1,0:T(8,128)(2,1)S(1)} %bitcast.74, bf16[16,512,128]{2,1,0:T(8,128)(2,1)} %bitcast.75), kind=kOutput, calls=%fused_computation.62 | convolution fusion | flops 1090519552 | bytes 21012480 | tf_op jit(solution)/shard_map/sub | solution.py:27
  250.6 8.9 %convert_bitcast_fusion.1 = bf16[16,64,8,128]{3,2,1,0:T(8,128)(2,1)S(1)} fusion(bf16[16,512,128]{2,1,0:T(8,128)(2,1)} %bitcast.76, f32[16,512,512]{1,2,0:T(8,128)} %get-tuple-element.11, f32[16,512]{1,0:T(8,128)S(1)} %get-tuple-element.10), kind=kOutput, calls=%fused_computation.28 | convolution fusion | flops 1083179008 | bytes 21004288 | tf_op jit(solution)/shard_map/cqk,ckd->cqd/dot_general | solution.py:29
  259.5 3.8 copy.78
  263.3 5.2 %all-to-all-start.2 = ((bf16[16,64,8,128]{3,0,2,1:T(8,128)(2,1)}), bf16[16,64,8,128]{3,0,2,1:T(8,128)(2,1)S(1)}, u32[]{:S(2)}, u32[]{:S(2)}) async-start(bf16[16,64,8,128]{3,0,2,1:T(8,128)(2,1)} %copy.78), calls=%async_computation.2 | async-start | bytes 4194304 | tf_op jit(solution)/shard_map/all_to_all | solution.py:69
  268.5 0.0 reduce-scatter.2.cloned.1.call-start
  268.6 0.3 convert_convert_fusion
  268.8 1.6 copy.80
  270.4 0.7 fusion.12
  271.1 48.8 %all-to-all-done.2 = bf16[16,64,8,128]{3,0,2,1:T(8,128)(2,1)S(1)} async-done(((bf16[16,64,8,128]{3,0,2,1:T(8,128)(2,1)}), bf16[16,64,8,128]{3,0,2,1:T(8,128)(2,1)S(1)}, u32[]{:S(2)}, u32[]{:S(2)}) %all-to-all-start.2) | async-done | bytes 2097184 | tf_op jit(solution)/shard_map/all_to_all | solution.py:69
  319.9 1.4 copy.79
  321.2 2.6 fusion.25
  323.8 0.7 copy.82
  324.6 9.5 %convolution_convert_fusion = bf16[512,4096]{1,0:T(8,128)(2,1)} fusion(bf16[1024,4096]{0,1:T(8,128)(2,1)} %all-gather.2.cloned.1.call-done, bf16[64,8,8,128]{3,2,1,0:T(8,128)(2,1)S(1)} %bitcast.79), kind=kOutput, calls=%fused_computation.10 | convolution fusion | flops 4297064448 | bytes 13631488 | tf_op jit(solution)/shard_map/dot_general | solution.py:77
  334.1 43.6 %reduce-scatter.2.cloned.1.call-done = bf16[512,1024]{1,0:T(8,128)(2,1)} async-done(((bf16[512,4096]{1,0:T(8,128)(2,1)}), bf16[512,1024]{1,0:T(8,128)(2,1)}) %reduce-scatter.2.cloned.1.call-update) | async-done | bytes 1048592 | tf_op jit(solution)/shard_map/reduce_scatter | solution.py:82
  (27 shorter events, 0.2 us)
Async XLA Ops:
  6.5 0.8 copy-start
  6.5 15.1 %copy-start.2 = (bf16[128,4096]{1,0:T(8,128)(2,1)S(1)}, bf16[128,4096]{1,0:T(8,128)(2,1)}, u32[]{:S(2)}) copy-start(bf16[128,4096]{1,0:T(8,128)(2,1)} %param.5) | copy-start | bytes 3145732
  8.5 41.7 %all-to-all-start = ((s32[64,8,512]{2,1,0:T(8,128)}), s32[64,8,512]{2,1,0:T(8,128)S(1)}, u32[]{:S(2)}, u32[]{:S(2)}) async-start(s32[64,8,512]{2,1,0:T(8,128)} %stack.7), calls=%async_computation | async-start | bytes 2097152 | tf_op jit(solution)/shard_map/all_to_all | solution.py:57
  22.4 1.3 copy-start.3
  24.4 1.3 copy-start.4
  27.7 1.2 copy-start.5
  27.7 1.5 copy-start.6
  27.7 1.9 copy-start.7
  50.2 177.9 %all-to-all-start.1 = ((bf16[3,256,16,2,128]{4,2,3,0,1:T(8,128)(2,1)}), bf16[3,256,16,2,128]{4,2,3,0,1:T(8,128)(2,1)}, u32[]{:S(2)}, u32[]{:S(2)}) async-start(bf16[3,256,16,2,128]{4,2,3,0,1:T(8,128)(2,1)} %copy.73), calls=%async_computation.1 | async-start | bytes 12582912 | tf_op jit(solution)/shard_map/all_to_all | solution.py:53
  59.8 264.8 %all-gather.2.cloned.1.call-start = ((), (), s32[]{:S(2)}) async-start(), calls=%async_computation.4 | async-start | bytes 8519680 | tf_op jit(solution)/shard_map/all_gather | solution.py:79
  263.3 56.6 %all-to-all-start.2 = ((bf16[16,64,8,128]{3,0,2,1:T(8,128)(2,1)}), bf16[16,64,8,128]{3,0,2,1:T(8,128)(2,1)S(1)}, u32[]{:S(2)}, u32[]{:S(2)}) async-start(bf16[16,64,8,128]{3,0,2,1:T(8,128)(2,1)} %copy.78), calls=%async_computation.2 | async-start | bytes 4194304 | tf_op jit(solution)/shard_map/all_to_all | solution.py:69
  268.5 109.1 %reduce-scatter.2.cloned.1.call-start = ((), (), s32[]{:S(2)}) async-start(), calls=%async_computation.5 | async-start | bytes 5242880 | tf_op jit(solution)/shard_map/reduce_scatter | solution.py:82
  271.1 50.1 %copy-start.8 = (bf16[8,4,128,128]{3,2,0,1:T(8,128)(2,1)S(1)}, bf16[8,4,128,128]{3,2,0,1:T(8,128)(2,1)}, u32[]{:S(2)}) copy-start(bf16[8,4,128,128]{3,2,0,1:T(8,128)(2,1)} %copy.80) | copy-start | bytes 3145732
  334.0 43.6 %copy-start.1 = (s32[32,512,1]{1,2,0:T(1,128)S(1)}, s32[32,512,1]{1,2,0:T(1,128)}, u32[]{:S(2)}) copy-start(s32[32,512,1]{1,2,0:T(1,128)} %param.8) | copy-start | bytes 196612
Sparse Core Ops, SparseCore 0:
  63.4 139.8 all-gather.1
  334.2 43.4 reduce-scatter.1
